TPU v7x, 128 devices: a whole 4x4x4 slice. The times are simulated.
128 devices in a mesh: seq: 32 (over x, y, core), wa: 4 (over z).
Axes of the slice: x: 4, y: 4, z: 4, core: 2. Of those that a mesh axis runs over, the one named last changes fastest.
Arguments:
- hidden_in: bfloat16 [16384, 2048], P('seq', 'wa'), may hold values from -6 to 6
- request_spans: int32 [4, 2], replicated, may hold values from 0 to 16384, as said below
- owners: int32 [4], replicated, may hold values from 0 to 31, as said below
- mixer_gain: float32 [2048], replicated, may hold values from 0.1 to 1.9
- query_weight: bfloat16 [2048, 2048], P(None, 'wa'), may hold values from -0.125 to 0.125
- forget_weight: bfloat16 [2048, 2048], P(None, 'wa'), may hold values from -0.0625 to 0.0625
- input_weight: bfloat16 [2048, 2048], P(None, 'wa'), may hold values from -0.125 to 0.125
- gate_weight: bfloat16 [2048, 2048], P(None, 'wa'), may hold values from -0.125 to 0.125
- forget_bias: float32 [2048], P('wa')
- output_weight: bfloat16 [2048, 2048], P('wa'), may hold values from -0.125 to 0.125
- swiglu_gain: float32 [2048], replicated, may hold values from 0.1 to 1.9
- swiglu_gate: bfloat16 [2048, 3072], P(None, 'wa'), may hold values from -0.125 to 0.125
- swiglu_up: bfloat16 [2048, 3072], P(None, 'wa'), may hold values from -0.125 to 0.125
- swiglu_down: bfloat16 [3072, 2048], P('wa'), may hold values from -0.109375 to 0.109375
Outputs:
- hidden_out: bfloat16 [16384, 2048], P('seq', 'wa')
- handed_state: float32 [32, 16, 128, 128], P('seq', 'wa')
Inputs may be any that keep to these rules, and one draw needn't show every extreme that they name: Requests lie back to back in order: request_spans[0, 0] = 0, each request's end equals the next one's start, the last end is 16384, and every request holds at least 64 tokens. The owners are distinct indices along seq; the last request's owner is the index half of 32 minus one; the first request's owner is the index just before that of the device holding the first request's last token, counted round; the index 31 is always an owner.
All inputs are finite; a program needn't handle non-finite values.
Results may differ from a plain program's by a relative error of at most 0.009.
Values may be sent and summed in bfloat16 or wider, within the bound.
No kernel may reach another device: no remote copies, remote signals or barrier semaphores. Data moves between devices by JAX's collectives and lax.ppermute only.
A program may use at most 128 MiB of HBM per device.

v0:
```python
import jax
import jax.numpy as jnp
from jax import lax
from jax.sharding import PartitionSpec as P

HEAD = 128
GROUP = 64
REQS = 4


EPS = 1e-06
HIGH = lax.Precision.HIGH


def hi_lo(values):
    high = values.astype(jnp.bfloat16)
    return high, (values - high.astype(jnp.float32)).astype(jnp.bfloat16)


def entering(decay, state, axis, targets):
    count = lax.axis_size(axis)
    rows = state.shape[1]
    high, low = hi_lo(decay)
    packed = jnp.concatenate([state.astype(jnp.bfloat16), high[:, None, :], low[:, None, :]], axis=1)
    every = lax.all_gather(packed, axis)
    decays = every[:, :, rows].astype(jnp.float32) + every[:, :, rows + 1].astype(jnp.float32)
    states = every[:, :, :rows].astype(jnp.float32)
    ranks = jnp.arange(count, dtype=jnp.int32)
    results = []
    for target in targets:
        between = (ranks[None, :] > ranks[:, None]) & (ranks[None, :] < target)
        weights = jnp.prod(jnp.where(between[:, :, None, None], decays[None], 1.0), axis=1)
        weights = jnp.where((ranks < target)[:, None, None], weights, 0.0)
        results.append(jnp.sum(weights[..., None] * states, axis=0))
    return results


def route_packets(packets, end_rows, owners, tok_rows, axis):
    count, mine = (lax.axis_size(axis), lax.axis_index(axis))
    left = [(i, (i - 1) % count) for i in range(count)]
    first = lax.ppermute(packets[0], axis, left)
    last = lax.ppermute(packets[-1], axis, [(count - 1, count // 2 - 1)])
    middle = packets[1:-1]
    place = ((end_rows - 1) // tok_rows)[1:-1]
    offset = (owners[1:-1] - place) % count
    for bit in range((count - 1).bit_length()):
        stride = 1 << bit
        moving = ((offset >> bit) & 1) == 1
        go = (moving & (place == mine))[:, None, None, None]
        sent = jnp.where(go, middle, jnp.zeros_like(middle))
        got = lax.ppermute(sent, axis, [(i, (i + stride) % count) for i in range(count)])
        middle = jnp.where(go, jnp.zeros_like(middle), middle) + got
        place = jnp.where(moving, (place + stride) % count, place)
    zero = jnp.zeros_like(first)
    held = jnp.where(owners[0] == mine, first, zero) + jnp.where(owners[-1] == mine, last, zero)
    return held + jnp.sum(middle, axis=0)


def rms_rows(matrix, scaling):
    matrix = matrix.astype(jnp.float32)
    rescale = lax.rsqrt(jnp.mean(matrix * matrix, axis=-1, keepdims=True) + EPS)
    return (matrix * rescale * scaling).astype(jnp.bfloat16)


def project(matrix, weight):
    return jnp.dot(matrix, weight, preferred_element_type=jnp.float32)


def widen_rows(shard_part):
    return lax.all_gather(shard_part, "wa", axis=1, tiled=True)


def narrow_sum(partial_terms):
    rows, cols = partial_terms.shape
    count = lax.axis_size("wa")
    pieces = partial_terms.astype(jnp.bfloat16).reshape(rows, count, cols // count)
    got = lax.all_to_all(pieces, "wa", 1, 1)
    return jnp.sum(got.astype(jnp.float32), axis=1)


def local(
    hidden_in,
    request_spans,
    owners,
    mixer_gain,
    query_weight,
    forget_weight,
    input_weight,
    gate_weight,
    forget_bias,
    output_weight,
    swiglu_gain,
    swiglu_gate,
    swiglu_up,
    swiglu_down,
):
    tok_rows = hidden_in.shape[0]
    head_count = query_weight.shape[1] // HEAD
    block_count = tok_rows // GROUP
    gathered = widen_rows(hidden_in)
    normed = rms_rows(gathered, mixer_gain)
    queries = jax.nn.silu(project(normed, query_weight))
    forget_logit = project(normed, forget_weight) + forget_bias
    log_decay = jax.nn.log_sigmoid(forget_logit)
    key_rows = jax.nn.sigmoid(-forget_logit)
    value_rows = project(normed, input_weight)
    gate_logit = project(normed, gate_weight)
    first_row = lax.axis_index("seq") * tok_rows
    position = first_row + jnp.arange(tok_rows, dtype=jnp.int32)
    start_rows = request_spans[:, 0]
    end_rows = request_spans[:, 1]
    is_start = jnp.any(position[:, None] == start_rows[None, :], axis=1)
    segment = jnp.sum((start_rows[None, :] <= position[:, None]).astype(jnp.int32), axis=1) - 1
    shape_four = (block_count, GROUP, head_count, HEAD)
    query_parts = queries.reshape(shape_four)
    key_parts = key_rows.reshape(shape_four)
    value_parts = value_rows.reshape(shape_four)
    segment_parts = segment.reshape(block_count, GROUP)
    keep_mask = (1.0 - is_start.astype(jnp.float32)).reshape(block_count, GROUP)
    cum_decay = jnp.cumsum(log_decay.reshape(shape_four), axis=1)
    surviving = jnp.cumprod(keep_mask, axis=1)
    query_tilde = query_parts * jnp.exp(cum_decay)
    key_tilde = key_parts * jnp.exp(-cum_decay)
    offsets = jnp.arange(GROUP, dtype=jnp.int32)
    causal = offsets[:, None] >= offsets[None, :]
    same_doc = causal[None] & (segment_parts[:, :, None] == segment_parts[:, None, :])
    scores = jnp.einsum("nihc,njhc->nhij", query_tilde, key_tilde, precision=HIGH)
    scores = jnp.where(same_doc[:, None], scores, 0.0)
    inner_out = jnp.einsum("nhij,njhd->nihd", scores, value_parts, precision=HIGH)
    tail_mask = (segment_parts == segment_parts[:, -1:]).astype(jnp.float32)
    last_decay = jnp.exp(cum_decay[:, -1])
    fresh = last_decay[..., None] * jnp.einsum(
        "njhc,njhd->nhcd", key_tilde * tail_mask[:, :, None, None], value_parts, precision=HIGH
    )
    shrink = surviving[:, -1][:, None, None] * last_decay

    def advance(carried, blocked):
        running, product = carried
        shrink_part, fresh_part = blocked
        return (
            (shrink_part[..., None] * running + fresh_part, product * shrink_part),
            (running, product),
        )

    initial = (
        jnp.zeros((head_count, HEAD, HEAD), jnp.float32),
        jnp.ones((head_count, HEAD), jnp.float32),
    )
    (local_state, device_decay), (start_state, start_decay) = lax.scan(
        advance, initial, (shrink, fresh), unroll=True
    )

    packets = []
    for request in range(REQS):
        local_end = end_rows[request] - 1 - first_row
        inside = (local_end >= 0) & (local_end < tok_rows)
        end_row = jnp.clip(local_end, 0, tok_rows - 1)
        block_index = end_row // GROUP
        within = end_row % GROUP
        decay_block = lax.dynamic_index_in_dim(cum_decay, block_index, 0, keepdims=False)
        key_block = lax.dynamic_index_in_dim(key_tilde, block_index, 0, keepdims=False)
        value_block = lax.dynamic_index_in_dim(value_parts, block_index, 0, keepdims=False)
        segment_block = lax.dynamic_index_in_dim(segment_parts, block_index, 0, keepdims=False)
        alive_block = lax.dynamic_index_in_dim(surviving, block_index, 0, keepdims=False)
        start_block = lax.dynamic_index_in_dim(start_state, block_index, 0, keepdims=False)
        carry_block = lax.dynamic_index_in_dim(start_decay, block_index, 0, keepdims=False)
        decay_end = lax.dynamic_index_in_dim(decay_block, within, 0, keepdims=False)
        segment_end = lax.dynamic_index_in_dim(segment_block, within, 0, keepdims=False)
        alive_end = lax.dynamic_index_in_dim(alive_block, within, 0, keepdims=False)
        upto_mask = ((offsets <= within) & (segment_block == segment_end)).astype(jnp.float32)
        partial_end = jnp.einsum(
            "jhc,jhd->hcd", key_block * upto_mask[:, None, None], value_block, precision=HIGH
        )
        grow = jnp.exp(decay_end)
        local_part = grow[..., None] * (alive_end * start_block + partial_end)
        high, low = hi_lo(grow * alive_end * carry_block)
        packet = jnp.concatenate(
            [local_part.astype(jnp.bfloat16), high[:, None, :], low[:, None, :]], axis=1
        )
        packets.append(jnp.where(inside, packet, jnp.zeros_like(packet)))
    held = route_packets(jnp.stack(packets), end_rows, owners, tok_rows, "seq")
    mine = lax.axis_index("seq")
    owned_source = jnp.sum(jnp.where(owners == mine, (end_rows - 1) // tok_rows, 0))
    incoming, owned_incoming = entering(device_decay, local_state, "seq", (mine, owned_source))
    held_coeff = held[:, HEAD].astype(jnp.float32) + held[:, HEAD + 1].astype(jnp.float32)
    handed_state = (held[:, :HEAD].astype(jnp.float32) + held_coeff[..., None] * owned_incoming)[None]
    block_state = start_state + start_decay[..., None] * incoming[None]
    carried_out = jnp.einsum("nihc,nhcd->nihd", query_tilde, block_state, precision=HIGH)
    mixer_out = (inner_out + surviving[:, :, None, None] * carried_out).reshape(
        tok_rows, head_count, HEAD
    )
    rescale = lax.rsqrt(jnp.mean(mixer_out * mixer_out, axis=-1, keepdims=True) + EPS)
    gate_heads = jax.nn.silu(gate_logit.reshape(tok_rows, head_count, HEAD))
    mixed_rows = (
        (mixer_out * rescale * gate_heads).reshape(tok_rows, head_count * HEAD).astype(jnp.bfloat16)
    )
    partial_terms = project(mixed_rows, output_weight)
    residual = (hidden_in.astype(jnp.float32) + narrow_sum(partial_terms)).astype(jnp.bfloat16)
    widened = widen_rows(residual)
    normed_ffn = rms_rows(widened, swiglu_gain)
    hidden = (
        jax.nn.silu(project(normed_ffn, swiglu_gate)) * project(normed_ffn, swiglu_up)
    ).astype(jnp.bfloat16)
    hidden_out = (residual.astype(jnp.float32) + narrow_sum(project(hidden, swiglu_down))).astype(
        jnp.bfloat16
    )
    return (hidden_out, handed_state)


def solution(mesh):
    in_specs = (
        P("seq", "wa"),
        P(),
        P(),
        P(),
        P(None, "wa"),
        P(None, "wa"),
        P(None, "wa"),
        P(None, "wa"),
        P("wa"),
        P("wa", None),
        P(),
        P(None, "wa"),
        P(None, "wa"),
        P("wa", None),
    )
    out_specs = (P("seq", "wa"), P("seq", "wa", None, None))
    return jax.shard_map(local, mesh=mesh, in_specs=in_specs, out_specs=out_specs, check_vma=False)
```

profile of v0, /device:TPU:0, one launch (start us, length us, event | category | flops | bytes accessed | tf_op | source)
XLA Modules:
  0.0 289.6 jit_solution(10031101498161709814)
XLA Ops:
  9.9 33.3 %all-gather.5.cloned.1.call-done = bf16[512,2048]{1,0:T(8,128)(2,1)} async-done(((bf16[512,512]{1,0:T(8,128)(2,1)}), bf16[512,2048]{1,0:T(8,128)(2,1)}) %all-gather.5.cloned.1.call-update) | async-done | bytes 2097168 | tf_op jit(solution)/shard_map/all_gather | solution.py:70
  45.5 4.9 %add_divide_fusion = (f32[512,512]{1,0:T(8,128)}, f32[512,512]{1,0:T(8,128)}) fusion(f32[512]{0:T(512)S(1)} %copy-done.26, bf16[2048,512]{1,0:T(8,128)(2,1)} %param.19, bf16[512,2048]{1,0:T(8,128)(2,1)S(1)} %copy-done.11, f32[2048]{0:T(1024)S(1)} %copy-done.25, f32[512]{0:T(512)S(1)} %add_rsqrt_fusion.1), kind=kOutput, calls=%fused_computation.62 | convolution fusion | flops 1080819712 | bytes 6303744 | tf_op jit(solution)/shard_map/dot_general | solution.py:66
  50.4 2.5 reshape.795
  55.5 4.7 %divide_multiply_fusion = f32[512,512]{1,0:T(8,128)} fusion(bf16[2048,512]{1,0:T(8,128)(2,1)} %param.18, bf16[512,2048]{1,0:T(8,128)(2,1)} %all-gather.5.cloned.1.call-done, f32[2048]{0:T(1024)S(1)} %copy-done.25, f32[512]{0:T(512)S(1)} %add_rsqrt_fusion.1), kind=kOutput, calls=%fused_computation.63 | convolution fusion | flops 1078984704 | bytes 5253120 | tf_op jit(solution)/shard_map/dot_general | solution.py:66
  62.7 4.9 %broadcast_multiply_fusion = (f32[8,64,4,128]{3,0,1,2:T(8,128)}, f32[8,64,4,128]{3,0,1,2:T(8,128)}, f32[8,64,4,128]{3,0,1,2:T(8,128)}, f32[8,64,4,128]{3,0,1,2:T(8,128)S(1)}) fusion(f32[8,64]{0,1:T(8,128)S(1)} %copy.162, f32[8,64,4,128]{3,2,1,0:T(4,128)} %reshape.796, f32[8,64,4,128]{3,2,1,0:T(4,128)} %reshape.794, f32[8,64,4,128]{3,2,1,0:T(4,128)} %reshape.795), kind=kOutput, calls=%fused_computation.69 | output fusion | flops 17563648 | bytes 7342080 | tf_op jit(solution)/shard_map/jit(cumsum)/reduce_window_sum | solution.py:120
  73.6 3.8 %convolution_multiply_fusion = f32[8,4,128,128]{3,2,1,0:T(8,128)S(1)} fusion(f32[8,64,4,128]{3,0,1,2:T(8,128)} %get-tuple-element.31, f32[8,4,128]{2,1,0:T(4,128)S(1)} %bitcast.229, f32[8,64,4,128]{3,2,1,0:T(4,128)} %reshape.793), kind=kOutput, calls=%fused_computation.26 | convolution fusion | flops 201850880 | bytes 4210688 | tf_op jit(solution)/shard_map/njhc,njhd->nhcd/dot_general | solution.py:132
  89.4 37.3 %all-gather.9.cloned.1.call-done = bf16[128,130,128]{2,1,0:T(8,128)(2,1)} async-done(((bf16[4,130,128]{2,1,0:T(8,128)(2,1)}), bf16[128,130,128]{2,1,0:T(8,128)(2,1)}) %all-gather.9.cloned.1.call-update) | async-done | bytes 4259856 | tf_op jit(solution)/shard_map/all_gather | solution.py:25
  129.1 8.3 %fusion.1 = (f32[4,128,128]{2,1,0:T(8,128)}, f32[4,128,128]{2,1,0:T(8,128)S(1)}) fusion(f32[32,4,128]{2,1,0:T(4,128)S(1)} %broadcast_select_fusion.5, bf16[32,4,130,128]{3,2,1,0:T(8,128)(2,1)} %bitcast.218, f32[32,4,128]{2,1,0:T(4,128)S(1)} %broadcast_select_fusion.6), kind=kLoop, calls=%fused_computation.3 | loop fusion | flops 10354688 | bytes 4849664 | tf_op jit(solution)/shard_map/reduce_sum | solution.py:34
  140.8 2.9 %copy.167 = f32[8,64,4,128]{3,2,1,0:T(4,128)} copy(f32[8,64,4,128]{3,1,2,0:T(8,128)} %get-tuple-element.98) | data formatting | bytes 2097152 | tf_op jit(solution)/shard_map/add | solution.py:189
  145.3 7.3 %convolution_convert_fusion.1 = bf16[512,2048]{1,0:T(8,128)(2,1)} fusion(bf16[512,2048]{1,0:T(8,128)(2,1)} %param.23, f32[64,8,4,128]{3,2,1,0:T(4,128)} %bitcast.221, f32[64,8,4,128]{3,2,1,0:T(4,128)} %bitcast.223, bf16[2048,512]{1,0:T(8,128)(2,1)} %param.21, bf16[512,2048]{1,0:T(8,128)(2,1)} %all-gather.5.cloned.1.call-done, f32[2048]{0:T(1024)S(1)} %copy-done.25, ...), kind=kOutput, calls=%fused_computation.18 | convolution fusion | flops 2154561536 | bytes 10496000 | tf_op jit(solution)/shard_map/dot_general | solution.py:66
  152.6 3.1 %copy.243 = bf16[64,4,8,512]{3,2,0,1:T(8,128)(2,1)} copy(bf16[64,4,8,512]{3,2,1,0:T(8,128)(2,1)} %bitcast.219) | data formatting | bytes 4194304 | tf_op jit(solution)/shard_map/reshape | solution.py:76
  155.7 4.5 %all-to-all-start = ((bf16[512,4,512]{2,0,1:T(8,128)(2,1)}), bf16[512,4,512]{2,0,1:T(8,128)(2,1)}, u32[]{:S(2)}, u32[]{:S(2)}) async-start(bf16[512,4,512]{2,0,1:T(8,128)(2,1)} %bitcast.215), calls=%async_computation | async-start | bytes 4194304 | tf_op jit(solution)/shard_map/all_to_all | solution.py:77
  168.3 18.9 %all-to-all-done = bf16[512,4,512]{2,0,1:T(8,128)(2,1)} async-done(((bf16[512,4,512]{2,0,1:T(8,128)(2,1)}), bf16[512,4,512]{2,0,1:T(8,128)(2,1)}, u32[]{:S(2)}, u32[]{:S(2)}) %all-to-all-start) | async-done | bytes 2097184 | tf_op jit(solution)/shard_map/all_to_all | solution.py:77
  190.3 3.1 %fusion.87 = (f32[64]{0:T(128)S(1)}, f32[64]{0:T(128)S(1)}, f32[64]{0:T(128)S(1)}, f32[64]{0:T(128)}) fusion(s32[8,64]{1,0:T(8,128)S(1)} %sub.138, s32[]{:T(128)S(6)} %select_n.278, s32[]{:T(128)} %bitcast.29, s32[]{:T(128)S(6)} %select_n.280, s32[]{:T(128)} %bitcast.64, s32[]{:T(128)S(6)} %select_n.315, s32[]{:T(128)S(6)} %select_n.317, s32[]{:T(128)} %bitcast.51, ...), kind=kLoop, calls=%fused_computation.221 | loop fusion | flops 1024 | bytes 2096 | tf_op jit(solution)/shard_map/convert_element_type | solution.py:170
  195.7 3.0 %constant_dynamic-slice_fusion.18 = (f32[1,64,4,128]{3,0,1,2:T(1,128)S(1)}, f32[1,64,4,128]{3,0,1,2:T(1,128)S(1)}, f32[1,64,4,128]{3,0,1,2:T(1,128)S(1)}, f32[1,64,4,128]{3,0,1,2:T(1,128)S(1)}) fusion(f32[8,64,4,128]{3,0,1,2:T(8,128)} %get-tuple-element.32, s32[]{:T(128)S(6)} %select_n.278, s32[]{:T(128)S(6)} %select_n.307, s32[]{:T(128)S(6)} %select_n.288, ...), kind=kLoop, calls=%fused_computation.180 | loop fusion | bytes 1048592 | tf_op jit(solution)/shard_map/jit(dynamic_index_in_dim)/dynamic_slice | solution.py:161
  206.9 7.4 %collective-permute-done.2 = bf16[2,4,130,128]{3,2,1,0:T(8,128)(2,1)S(1)} collective-permute-done((bf16[2,4,130,128]{3,2,1,0:T(8,128)(2,1)S(1)}, bf16[2,4,130,128]{3,2,1,0:T(8,128)(2,1)S(1)}, u32[]{:S(2)}, u32[]{:S(2)}) %collective-permute-start.2) | collective-permute-done | bytes 266272 | tf_op jit(solution)/shard_map/ppermute | solution.py:51
  216.5 8.9 %collective-permute-done.3 = bf16[2,4,130,128]{3,2,1,0:T(8,128)(2,1)S(1)} collective-permute-done((bf16[2,4,130,128]{3,2,1,0:T(8,128)(2,1)S(1)}, bf16[2,4,130,128]{3,2,1,0:T(8,128)(2,1)S(1)}, u32[]{:S(2)}, u32[]{:S(2)}) %collective-permute-start.3) | collective-permute-done | bytes 266272 | tf_op jit(solution)/shard_map/ppermute | solution.py:51
  227.6 8.2 %collective-permute-done.4 = bf16[2,4,130,128]{3,2,1,0:T(8,128)(2,1)S(1)} collective-permute-done((bf16[2,4,130,128]{3,2,1,0:T(8,128)(2,1)S(1)}, bf16[2,4,130,128]{3,2,1,0:T(8,128)(2,1)S(1)}, u32[]{:S(2)}, u32[]{:S(2)}) %collective-permute-start.4) | collective-permute-done | bytes 266272 | tf_op jit(solution)/shard_map/ppermute | solution.py:51
  240.1 5.0 %fusion.40 = f32[512,768]{1,0:T(8,128)} fusion(bf16[2048,768]{1,0:T(8,128)(2,1)} %param.25, bf16[512,2048]{1,0:T(8,128)(2,1)S(1)} %copy-done.13, f32[2048]{0:T(1024)} %param.24, f32[512]{0:T(512)S(1)} %add_rsqrt_fusion), kind=kOutput, calls=%fused_computation.68 | convolution fusion | flops 1614807040 | bytes 6825984 | tf_op jit(solution)/shard_map/dot_general | solution.py:66
  245.0 8.3 %convolution_convert_fusion = bf16[512,2048]{1,0:T(8,128)(2,1)} fusion(bf16[768,2048]{1,0:T(8,128)(2,1)S(1)} %copy-done, f32[512,768]{1,0:T(8,128)} %fusion.40, bf16[2048,768]{1,0:T(8,128)(2,1)} %param.26, bf16[512,2048]{1,0:T(8,128)(2,1)} %all-gather.7.cloned.1.call-done, f32[2048]{0:T(1024)} %param.24, f32[512]{0:T(512)} %copy-done.23), kind=kOutput, calls=%fused_computation.17 | convolution fusion | flops 3228827648 | bytes 12068864 | tf_op jit(solution)/shard_map/dot_general | solution.py:66
  253.3 3.1 %copy.242 = bf16[64,4,8,512]{3,2,0,1:T(8,128)(2,1)} copy(bf16[64,4,8,512]{3,2,1,0:T(8,128)(2,1)} %bitcast.220) | data formatting | bytes 4194304 | tf_op jit(solution)/shard_map/reshape | solution.py:76
  256.5 4.5 %all-to-all-start.1 = ((bf16[512,4,512]{2,0,1:T(8,128)(2,1)}), bf16[512,4,512]{2,0,1:T(8,128)(2,1)}, u32[]{:S(2)}, u32[]{:S(2)}) async-start(bf16[512,4,512]{2,0,1:T(8,128)(2,1)} %bitcast.216), calls=%async_computation.1 | async-start | bytes 4194304 | tf_op jit(solution)/shard_map/all_to_all | solution.py:77
  265.7 6.6 %collective-permute-done.6 = bf16[2,4,130,128]{3,2,1,0:T(8,128)(2,1)S(1)} collective-permute-done((bf16[2,4,130,128]{3,2,1,0:T(8,128)(2,1)S(1)}, bf16[2,4,130,128]{3,2,1,0:T(8,128)(2,1)S(1)}, u32[]{:S(2)}, u32[]{:S(2)}) %collective-permute-start.6) | collective-permute-done | bytes 266272 | tf_op jit(solution)/shard_map/ppermute | solution.py:51
  274.5 5.6 %all-to-all-done.1 = bf16[512,4,512]{2,0,1:T(8,128)(2,1)} async-done(((bf16[512,4,512]{2,0,1:T(8,128)(2,1)}), bf16[512,4,512]{2,0,1:T(8,128)(2,1)}, u32[]{:S(2)}, u32[]{:S(2)}) %all-to-all-start.1) | async-done | bytes 2097184 | tf_op jit(solution)/shard_map/all_to_all | solution.py:77
  (171 shorter events, 71.1 us)
Async XLA Ops:
  7.2 237.9 %copy-start = (bf16[768,2048]{1,0:T(8,128)(2,1)S(1)}, bf16[768,2048]{1,0:T(8,128)(2,1)}, u32[]{:S(2)}) copy-start(bf16[768,2048]{1,0:T(8,128)(2,1)} %param.27) | copy-start | bytes 9437188
  7.2 38.3 %copy-start.25 = (f32[2048]{0:T(1024)S(1)}, f32[2048]{0:T(1024)}, u32[]{:S(2)}) copy-start(f32[2048]{0:T(1024)} %param.17) | copy-start | bytes 24580
  7.2 38.3 %copy-start.26 = (f32[512]{0:T(512)S(1)}, f32[512]{0:T(512)}, u32[]{:S(2)}) copy-start(f32[512]{0:T(512)} %param.22) | copy-start | bytes 6148
  7.2 36.1 %all-gather.5.cloned.1.call-start = ((), (), s32[]{:S(2)}) async-start(), calls=%async_computation.2 | async-start | bytes 2621440 | tf_op jit(solution)/shard_map/all_gather | solution.py:70
  7.9 118.8 %all-gather.9.cloned.1.call-start = ((), (), s32[]{:S(2)}) async-start(), calls=%async_computation.4 | async-start | bytes 4595712 | tf_op jit(solution)/shard_map/all_gather | solution.py:25
  62.7 6.1 %copy-start.12 = (bf16[512,2048]{1,0:T(8,128)(2,1)S(1)}, bf16[512,2048]{1,0:T(8,128)(2,1)}, u32[]{:S(2)}) copy-start(bf16[512,2048]{1,0:T(8,128)(2,1)} %all-gather.5.cloned.1.call-done) | copy-start | bytes 6291460
  62.7 6.1 %copy-start.24 = (bf16[2048,512]{1,0:T(8,128)(2,1)S(1)}, bf16[2048,512]{1,0:T(8,128)(2,1)}, u32[]{:S(2)}) copy-start(bf16[2048,512]{1,0:T(8,128)(2,1)} %param.20) | copy-start | bytes 6291460
  68.7 126.9 %copy-start.17 = (f32[8,4,128]{2,1,0:T(4,128)}, f32[8,4,128]{2,1,0:T(4,128)S(1)}, u32[]{:S(2)}) copy-start(f32[8,4,128]{2,1,0:T(4,128)S(1)} %get-tuple-element.52) | copy-start | bytes 49156
  129.1 8.3 %copy-start.5 = (f32[8,64,4,128]{3,0,1,2:T(8,128)S(1)}, f32[8,64,4,128]{3,0,1,2:T(8,128)}, u32[]{:S(2)}) copy-start(f32[8,64,4,128]{3,0,1,2:T(8,128)} %get-tuple-element.45) | copy-start | bytes 3145732
  129.1 8.3 %copy-start.8 = (f32[8,4,128,128]{3,2,1,0:T(8,128)S(1)}, f32[8,4,128,128]{3,2,1,0:T(8,128)}, u32[]{:S(2)}) copy-start(f32[8,4,128,128]{3,2,1,0:T(8,128)} %copy-done.7) | copy-start | bytes 6291460
  155.7 31.5 %all-to-all-start = ((bf16[512,4,512]{2,0,1:T(8,128)(2,1)}), bf16[512,4,512]{2,0,1:T(8,128)(2,1)}, u32[]{:S(2)}, u32[]{:S(2)}) async-start(bf16[512,4,512]{2,0,1:T(8,128)(2,1)} %bitcast.215), calls=%async_computation | async-start | bytes 4194304 | tf_op jit(solution)/shard_map/all_to_all | solution.py:77
  160.2 77.0 %all-gather.7.cloned.1.call-start = ((), (), s32[]{:S(2)}) async-start(), calls=%async_computation.3 | async-start | bytes 2621440 | tf_op jit(solution)/shard_map/all_gather | solution.py:70
  168.3 57.1 %copy-start.18 = (pred[2]{0:T(512)(128)(4,1)}, pred[2]{0:T(512)(128)(4,1)S(1)}, u32[]{:S(2)}) copy-start(pred[2]{0:T(512)(128)(4,1)S(1)} %get-tuple-element.94) | copy-start | bytes 10
  168.3 57.1 %copy-start.22 = (pred[2]{0:T(512)(128)(4,1)}, pred[2]{0:T(512)(128)(4,1)S(1)}, u32[]{:S(2)}) copy-start(pred[2]{0:T(512)(128)(4,1)S(1)} %get-tuple-element.93) | copy-start | bytes 10
  204.7 31.1 %copy-start.19 = (pred[2]{0:T(512)(128)(4,1)S(1)}, pred[2]{0:T(512)(128)(4,1)}, u32[]{:S(2)}) copy-start(pred[2]{0:T(512)(128)(4,1)} %get-tuple-element.8) | copy-start | bytes 10
  204.9 9.4 %collective-permute-start.2 = (bf16[2,4,130,128]{3,2,1,0:T(8,128)(2,1)S(1)}, bf16[2,4,130,128]{3,2,1,0:T(8,128)(2,1)S(1)}, u32[]{:S(2)}, u32[]{:S(2)}) collective-permute-start(bf16[2,4,130,128]{3,2,1,0:T(8,128)(2,1)S(1)} %broadcast_select_fusion), channel_id=1, source_target_pairs={{0,4},{4,8},{8,12},{12,16},{16,20},{20,24},{24,28},{28,32},{32,36}... | collective-permute-start | bytes 798728 | tf_op jit(solution)/shard_map/ppermute | solution.py:51
  214.4 11.0 %collective-permute-start.3 = (bf16[2,4,130,128]{3,2,1,0:T(8,128)(2,1)S(1)}, bf16[2,4,130,128]{3,2,1,0:T(8,128)(2,1)S(1)}, u32[]{:S(2)}, u32[]{:S(2)}) collective-permute-start(bf16[2,4,130,128]{3,2,1,0:T(8,128)(2,1)S(1)} %get-tuple-element.13), channel_id=1, source_target_pairs={{0,8},{4,12},{8,16},{12,20},{16,24},{20,28},{24,32},{28,36},{32,40... | collective-permute-start | bytes 798728 | tf_op jit(solution)/shard_map/ppermute | solution.py:51
  225.5 10.2 %collective-permute-start.4 = (bf16[2,4,130,128]{3,2,1,0:T(8,128)(2,1)S(1)}, bf16[2,4,130,128]{3,2,1,0:T(8,128)(2,1)S(1)}, u32[]{:S(2)}, u32[]{:S(2)}) collective-permute-start(bf16[2,4,130,128]{3,2,1,0:T(8,128)(2,1)S(1)} %broadcast_select_fusion.2), channel_id=1, source_target_pairs={{0,16},{4,20},{8,24},{12,28},{16,32},{20,36},{24,40},{28,44},{32,4... | collective-permute-start | bytes 798728 | tf_op jit(solution)/shard_map/ppermute | solution.py:51
  226.3 47.3 %collective-permute-start = (bf16[4,130,128]{2,1,0:T(8,128)(2,1)}, bf16[4,130,128]{2,1,0:T(8,128)(2,1)}, u32[]{:S(2)}, u32[]{:S(2)}) collective-permute-start(bf16[4,130,128]{2,1,0:T(8,128)(2,1)} %maximum_select_fusion), channel_id=1, source_target_pairs={{0,124},{4,0},{8,4},{12,8},{16,12},{20,16},{24,20},{28,24},{32,28}... | collective-permute-start | bytes 399368 | tf_op jit(solution)/shard_map/ppermute | solution.py:41
  237.2 25.9 %collective-permute-start.5 = (bf16[2,4,130,128]{3,2,1,0:T(8,128)(2,1)}, bf16[2,4,130,128]{3,2,1,0:T(8,128)(2,1)}, u32[]{:S(2)}, u32[]{:S(2)}) collective-permute-start(bf16[2,4,130,128]{3,2,1,0:T(8,128)(2,1)} %get-tuple-element.6), channel_id=1, source_target_pairs={{0,32},{4,36},{8,40},{12,44},{16,48},{20,52},{24,56},{28,60},{32,6... | collective-permute-start | bytes 798728 | tf_op jit(solution)/shard_map/ppermute | solution.py:51
  256.5 23.6 %all-to-all-start.1 = ((bf16[512,4,512]{2,0,1:T(8,128)(2,1)}), bf16[512,4,512]{2,0,1:T(8,128)(2,1)}, u32[]{:S(2)}, u32[]{:S(2)}) async-start(bf16[512,4,512]{2,0,1:T(8,128)(2,1)} %bitcast.216), calls=%async_computation.1 | async-start | bytes 4194304 | tf_op jit(solution)/shard_map/all_to_all | solution.py:77
  260.9 12.7 %copy-start.16 = (f32[4,128,128]{2,1,0:T(8,128)S(1)}, f32[4,128,128]{2,1,0:T(8,128)}, u32[]{:S(2)}) copy-start(f32[4,128,128]{2,1,0:T(8,128)} %get-tuple-element.2) | copy-start | bytes 786436
  264.3 8.1 %collective-permute-start.6 = (bf16[2,4,130,128]{3,2,1,0:T(8,128)(2,1)S(1)}, bf16[2,4,130,128]{3,2,1,0:T(8,128)(2,1)S(1)}, u32[]{:S(2)}, u32[]{:S(2)}) collective-permute-start(bf16[2,4,130,128]{3,2,1,0:T(8,128)(2,1)S(1)} %broadcast_select_fusion.4), channel_id=1, source_target_pairs={{0,64},{4,68},{8,72},{12,76},{16,80},{20,84},{24,88},{28,92},{32,9... | collective-permute-start | bytes 798728 | tf_op jit(solution)/shard_map/ppermute | solution.py:51
  265.1 8.5 %collective-permute-start.1 = (bf16[4,130,128]{2,1,0:T(8,128)(2,1)S(1)}, bf16[4,130,128]{2,1,0:T(8,128)(2,1)S(1)}, u32[]{:S(2)}, u32[]{:S(2)}) collective-permute-start(bf16[4,130,128]{2,1,0:T(8,128)(2,1)S(1)} %maximum_select_fusion.1), channel_id=1, source_target_pairs={{124,60},{125,61},{126,62},{127,63}} | collective-permute-start | bytes 399368 | tf_op jit(solution)/shard_map/ppermute | solution.py:42
  (15 other events, 31.4 us)
Sparse Core Ops, SparseCore 0:
  9.7 33.5 all-gather.4
  80.3 46.3 all-gather.8
  190.4 28.5 all-gather.6
where the time goes:
time: 292 us; the launch traced here: 290 us
  waiting for transfers between devices  127 us (43%)
  matrix products  50 us (17%)
  other arithmetic  48.4 us (17%)
  local copies, waits for them, and re-layouts  35.7 us (12%)
  between operations  18.4 us (6%)
  starting transfers between devices  10.2 us (3%)
    all_gather x1, waiting for transfers between devices, entering(): every = lax.all_gather(packed, axis)  37.3 us
    all_gather x2, waiting for transfers between devices, widen_rows(): return lax.all_gather(shard_part, 'wa', axis=1, tiled=True)  33.3 us
    dot_general x6, matrix products, project(): return jnp.dot(matrix, weight, preferred_element_type=jnp.float32)  32.4 us
    ppermute x5, waiting for transfers between devices, route_packets(): lax.ppermute(sent, axis, [(i, (i + stride) % count) for i in range(count)])  31.1 us
    all_to_all x2, waiting for transfers between devices, narrow_sum(): got = lax.all_to_all(pieces, 'wa', 1, 1)  24.5 us
    all_to_all x2, starting transfers between devices, narrow_sum(): got = lax.all_to_all(pieces, 'wa', 1, 1)  8.9 us
    dot_general x4, matrix products, local(): jnp.einsum('jhc,jhd->hcd', key_block * upto_mask[:, None, None], value_bl...  8.52 us
    reduce_sum x1, other arithmetic, entering(): results.append(jnp.sum(weights[..., None] * states, axis=0))  8.31 us
  transfers between devices with their start and end apart: 12, of which 8 were waited for; matrix products, arithmetic and copies ran while one was open for 21% of the time, Pallas kernels for 0%

commit v1 on v0

--- a/solution.py
+++ b/solution.py
@@ -17,12 +17,12 @@
     return high, (values - high.astype(jnp.float32)).astype(jnp.bfloat16)
 
 
-def entering(decay, state, axis, targets):
+def entering(decay, state, axis, targets, companion):
     count = lax.axis_size(axis)
     rows = state.shape[1]
     high, low = hi_lo(decay)
     packed = jnp.concatenate([state.astype(jnp.bfloat16), high[:, None, :], low[:, None, :]], axis=1)
-    every = lax.all_gather(packed, axis)
+    every, companion = lax.optimization_barrier((lax.all_gather(packed, axis), companion))
     decays = every[:, :, rows].astype(jnp.float32) + every[:, :, rows + 1].astype(jnp.float32)
     states = every[:, :, :rows].astype(jnp.float32)
     ranks = jnp.arange(count, dtype=jnp.int32)
@@ -32,7 +32,7 @@
         weights = jnp.prod(jnp.where(between[:, :, None, None], decays[None], 1.0), axis=1)
         weights = jnp.where((ranks < target)[:, None, None], weights, 0.0)
         results.append(jnp.sum(weights[..., None] * states, axis=0))
-    return results
+    return results, companion
 
 
 def route_packets(packets, end_rows, owners, tok_rows, axis):
@@ -181,7 +181,9 @@
     held = route_packets(jnp.stack(packets), end_rows, owners, tok_rows, "seq")
     mine = lax.axis_index("seq")
     owned_source = jnp.sum(jnp.where(owners == mine, (end_rows - 1) // tok_rows, 0))
-    incoming, owned_incoming = entering(device_decay, local_state, "seq", (mine, owned_source))
+    (incoming, owned_incoming), held = entering(
+        device_decay, local_state, "seq", (mine, owned_source), held
+    )
     held_coeff = held[:, HEAD].astype(jnp.float32) + held[:, HEAD + 1].astype(jnp.float32)
     handed_state = (held[:, :HEAD].astype(jnp.float32) + held_coeff[..., None] * owned_incoming)[None]
     block_state = start_state + start_decay[..., None] * incoming[None]

time: 292 us -> 295 us (1.010)
  blocking collectives: 0 us -> 20.6 us
  other arithmetic: 48.4 us -> 36.9 us
  waiting for transfers between devices: 127 us -> 132 us
  matrix products: 50 us -> 46 us
  starting transfers between devices: 10.2 us -> 6.54 us
    all_gather x1, waiting for transfers between devices: 37.3 us -> 0.02 us  [entering(): lax.all_gather(packed, axis)]
    all_gather x2, waiting for transfers between devices: 33.3 us -> 59.4 us  [widen_rows(): return lax.all_gather(shard_part, 'wa', axis=1, tiled=True)]
    all_to_all x0 -> x1, blocking collectives: none -> 20.6 us  [narrow_sum(): got = lax.all_to_all(pieces, 'wa', 1, 1)]
    ppermute x5, waiting for transfers between devices: 31.1 us -> 45.9 us  [route_packets(): lax.ppermute(sent, axis, [(i, (i + stride) % count) for i in range(count)])]
    all_to_all x2 -> x1, starting transfers between devices: 8.9 us -> 4.46 us  [narrow_sum(): got = lax.all_to_all(pieces, 'wa', 1, 1)]
    dot_general x4, matrix products: 8.52 us -> 4.46 us  [local(): jnp.einsum('jhc,jhd->hcd', key_block * upto_mask[:, None, None], value_bl...]
    all_to_all x2 -> x1, waiting for transfers between devices: 24.5 us -> 25.8 us  [narrow_sum(): got = lax.all_to_all(pieces, 'wa', 1, 1)]
  transfers between devices with their start and end apart: 12 -> 11, of which waited for: 8 -> 8; matrix products, arithmetic and copies ran while one was open for 21% -> 9% of each run, Pallas kernels for 0% -> 0%
where the time goes in v1:
time: 295 us; the launch traced here: 294 us
  waiting for transfers between devices  132 us (45%)
  matrix products  46 us (16%)
  other arithmetic  36.9 us (13%)
  local copies, waits for them, and re-layouts  33.6 us (11%)
  blocking collectives  20.6 us (7%)
  between operations  18.4 us (6%)
  starting transfers between devices  6.54 us (2%)
    all_gather x2, waiting for transfers between devices, widen_rows(): return lax.all_gather(shard_part, 'wa', axis=1, tiled=True)  59.4 us
    ppermute x5, waiting for transfers between devices, route_packets(): lax.ppermute(sent, axis, [(i, (i + stride) % count) for i in range(count)])  45.9 us
    dot_general x6, matrix products, project(): return jnp.dot(matrix, weight, preferred_element_type=jnp.float32)  32.5 us
    all_to_all x1, waiting for transfers between devices, narrow_sum(): got = lax.all_to_all(pieces, 'wa', 1, 1)  25.8 us
    all_to_all x1, blocking collectives, narrow_sum(): got = lax.all_to_all(pieces, 'wa', 1, 1)  20.6 us
    reduce_sum x1, other arithmetic, entering(): results.append(jnp.sum(weights[..., None] * states, axis=0))  7.61 us
  transfers between devices with their start and end apart: 11, of which 8 were waited for; matrix products, arithmetic and copies ran while one was open for 9% of the time, Pallas kernels for 0%

profile of v1, /device:TPU:0, one launch (start us, length us, event | category | flops | bytes accessed | tf_op | source)
XLA Modules:
  0.0 293.9 jit_solution(17448271470127059305)
XLA Ops:
  11.4 31.8 %all-gather.5.cloned.1.call-done = bf16[512,2048]{1,0:T(8,128)(2,1)} async-done(((bf16[512,512]{1,0:T(8,128)(2,1)}), bf16[512,2048]{1,0:T(8,128)(2,1)}) %all-gather.5.cloned.1.call-update) | async-done | bytes 2097168 | tf_op jit(solution)/shard_map/all_gather | solution.py:70
  45.5 4.9 %add_divide_fusion = (f32[512,512]{1,0:T(8,128)}, f32[512,512]{1,0:T(8,128)}) fusion(f32[512]{0:T(512)S(1)} %copy-done.23, bf16[2048,512]{1,0:T(8,128)(2,1)} %param.19, bf16[512,2048]{1,0:T(8,128)(2,1)S(1)} %copy-done.11, f32[2048]{0:T(1024)S(1)} %copy-done.22, f32[512]{0:T(512)S(1)} %add_rsqrt_fusion.1), kind=kOutput, calls=%fused_computation.62 | convolution fusion | flops 1080819712 | bytes 6303744 | tf_op jit(solution)/shard_map/dot_general | solution.py:66
  52.9 2.6 reshape.796
  55.5 4.6 %divide_multiply_fusion = f32[512,512]{1,0:T(8,128)} fusion(bf16[2048,512]{1,0:T(8,128)(2,1)} %param.18, bf16[512,2048]{1,0:T(8,128)(2,1)} %all-gather.5.cloned.1.call-done, f32[2048]{0:T(1024)S(1)} %copy-done.22, f32[512]{0:T(512)S(1)} %add_rsqrt_fusion.1), kind=kOutput, calls=%fused_computation.63 | convolution fusion | flops 1078984704 | bytes 5253120 | tf_op jit(solution)/shard_map/dot_general | solution.py:66
  60.2 2.5 reshape.794
  62.7 4.9 %broadcast_multiply_fusion = (f32[8,64,4,128]{3,0,1,2:T(8,128)}, f32[8,64,4,128]{3,0,1,2:T(8,128)}, f32[8,64,4,128]{3,0,1,2:T(8,128)}, f32[8,64,4,128]{3,0,1,2:T(8,128)S(1)}) fusion(f32[8,64]{0,1:T(8,128)S(1)} %copy.162, f32[8,64,4,128]{3,2,1,0:T(4,128)} %reshape.796, f32[8,64,4,128]{3,2,1,0:T(4,128)} %reshape.794, f32[8,64,4,128]{3,2,1,0:T(4,128)} %reshape.795), kind=kOutput, calls=%fused_computation.69 | output fusion | flops 17563648 | bytes 7342080 | tf_op jit(solution)/shard_map/jit(cumsum)/reduce_window_sum | solution.py:120
  71.1 2.5 reshape.793
  73.7 3.9 %convolution_multiply_fusion = f32[8,4,128,128]{3,2,1,0:T(8,128)S(1)} fusion(f32[8,64,4,128]{3,0,1,2:T(8,128)} %get-tuple-element.35, f32[8,4,128]{2,1,0:T(4,128)S(1)} %bitcast.229, f32[8,64,4,128]{3,2,1,0:T(4,128)} %reshape.793), kind=kOutput, calls=%fused_computation.26 | convolution fusion | flops 201850880 | bytes 4210688 | tf_op jit(solution)/shard_map/njhc,njhd->nhcd/dot_general | solution.py:132
  94.0 3.1 %constant_dynamic-slice_fusion.18 = (f32[1,64,4,128]{3,0,1,2:T(1,128)S(1)}, f32[1,64,4,128]{3,0,1,2:T(1,128)S(1)}, f32[1,64,4,128]{3,0,1,2:T(1,128)S(1)}, f32[1,64,4,128]{3,0,1,2:T(1,128)S(1)}) fusion(f32[8,64,4,128]{3,0,1,2:T(8,128)} %get-tuple-element.36, s32[]{:T(128)S(6)} %select_n.276, s32[]{:T(128)S(6)} %select_n.305, s32[]{:T(128)S(6)} %select_n.286, ...), kind=kLoop, calls=%fused_computation.178 | loop fusion | bytes 1048592 | tf_op jit(solution)/shard_map/jit(dynamic_index_in_dim)/dynamic_slice | solution.py:161
  102.7 7.4 %collective-permute-done.2 = bf16[2,4,130,128]{3,2,1,0:T(8,128)(2,1)S(1)} collective-permute-done((bf16[2,4,130,128]{3,2,1,0:T(8,128)(2,1)S(1)}, bf16[2,4,130,128]{3,2,1,0:T(8,128)(2,1)S(1)}, u32[]{:S(2)}, u32[]{:S(2)}) %collective-permute-start.2) | collective-permute-done | bytes 266272 | tf_op jit(solution)/shard_map/ppermute | solution.py:51
  110.9 17.1 %collective-permute-done.3 = bf16[2,4,130,128]{3,2,1,0:T(8,128)(2,1)S(1)} collective-permute-done((bf16[2,4,130,128]{3,2,1,0:T(8,128)(2,1)S(1)}, bf16[2,4,130,128]{3,2,1,0:T(8,128)(2,1)S(1)}, u32[]{:S(2)}, u32[]{:S(2)}) %collective-permute-start.3) | collective-permute-done | bytes 266272 | tf_op jit(solution)/shard_map/ppermute | solution.py:51
  129.9 8.6 %collective-permute-done.4 = bf16[2,4,130,128]{3,2,1,0:T(8,128)(2,1)S(1)} collective-permute-done((bf16[2,4,130,128]{3,2,1,0:T(8,128)(2,1)S(1)}, bf16[2,4,130,128]{3,2,1,0:T(8,128)(2,1)S(1)}, u32[]{:S(2)}, u32[]{:S(2)}) %collective-permute-start.4) | collective-permute-done | bytes 266272 | tf_op jit(solution)/shard_map/ppermute | solution.py:51
  139.5 7.0 %collective-permute-done.5 = bf16[2,4,130,128]{3,2,1,0:T(8,128)(2,1)S(1)} collective-permute-done((bf16[2,4,130,128]{3,2,1,0:T(8,128)(2,1)S(1)}, bf16[2,4,130,128]{3,2,1,0:T(8,128)(2,1)S(1)}, u32[]{:S(2)}, u32[]{:S(2)}) %collective-permute-start.5) | collective-permute-done | bytes 266272 | tf_op jit(solution)/shard_map/ppermute | solution.py:51
  149.0 5.9 %collective-permute-done.6 = bf16[2,4,130,128]{3,2,1,0:T(8,128)(2,1)S(1)} collective-permute-done((bf16[2,4,130,128]{3,2,1,0:T(8,128)(2,1)S(1)}, bf16[2,4,130,128]{3,2,1,0:T(8,128)(2,1)S(1)}, u32[]{:S(2)}, u32[]{:S(2)}) %collective-permute-start.6) | collective-permute-done | bytes 266272 | tf_op jit(solution)/shard_map/ppermute | solution.py:51
  157.7 7.6 %fusion.1 = (f32[4,128,128]{2,1,0:T(8,128)S(1)}, f32[4,128,128]{2,1,0:T(8,128)S(1)}) fusion(f32[32,4,128]{2,1,0:T(4,128)S(1)} %broadcast_select_fusion.5, bf16[32,4,130,128]{3,2,1,0:T(8,128)(2,1)} %bitcast.218, f32[32,4,128]{2,1,0:T(4,128)S(1)} %broadcast_select_fusion.6), kind=kLoop, calls=%fused_computation.3 | loop fusion | flops 10354688 | bytes 4849664 | tf_op jit(solution)/shard_map/reduce_sum | solution.py:34
  170.7 2.9 copy.177
  175.2 7.4 %convolution_convert_fusion.1 = bf16[512,2048]{1,0:T(8,128)(2,1)} fusion(bf16[512,2048]{1,0:T(8,128)(2,1)} %param.23, f32[64,8,4,128]{3,2,1,0:T(4,128)} %bitcast.221, f32[64,8,4,128]{3,2,1,0:T(4,128)} %bitcast.223, bf16[2048,512]{1,0:T(8,128)(2,1)} %param.21, bf16[512,2048]{1,0:T(8,128)(2,1)} %all-gather.5.cloned.1.call-done, f32[2048]{0:T(1024)} %param.17, ...), kind=kOutput, calls=%fused_computation.18 | convolution fusion | flops 2154561536 | bytes 10496000 | tf_op jit(solution)/shard_map/dot_general | solution.py:66
  184.4 20.6 %all_to_all.10 = bf16[512,4,512]{2,0,1:T(8,128)(2,1)S(1)} all-to-all(bf16[512,4,512]{2,0,1:T(8,128)(2,1)S(1)} %bitcast.216), channel_id=1, replica_groups=mesh['seq'=32,'wa'=4] {'wa'}, dimensions={1} | all-to-all | bytes 4194304 | tf_op jit(solution)/shard_map/all_to_all | solution.py:77
  207.0 27.6 %all-gather.7.cloned.1.call-done = bf16[512,2048]{1,0:T(8,128)(2,1)} async-done(((bf16[512,512]{1,0:T(8,128)(2,1)}), bf16[512,2048]{1,0:T(8,128)(2,1)}) %all-gather.7.cloned.1.call-update) | async-done | bytes 2097168 | tf_op jit(solution)/shard_map/all_gather | solution.py:70
  236.8 5.0 %fusion.40 = f32[512,768]{1,0:T(8,128)} fusion(bf16[2048,768]{1,0:T(8,128)(2,1)} %param.25, bf16[512,2048]{1,0:T(8,128)(2,1)S(1)} %copy-done.13, f32[2048]{0:T(1024)} %param.24, f32[512]{0:T(512)S(1)} %add_rsqrt_fusion), kind=kOutput, calls=%fused_computation.68 | convolution fusion | flops 1614807040 | bytes 6825984 | tf_op jit(solution)/shard_map/dot_general | solution.py:66
  241.8 8.3 %convolution_convert_fusion = bf16[512,2048]{1,0:T(8,128)(2,1)} fusion(bf16[768,2048]{1,0:T(8,128)(2,1)S(1)} %copy-done, f32[512,768]{1,0:T(8,128)} %fusion.40, bf16[2048,768]{1,0:T(8,128)(2,1)} %param.26, bf16[512,2048]{1,0:T(8,128)(2,1)} %all-gather.7.cloned.1.call-done, f32[2048]{0:T(1024)} %param.24, f32[512]{0:T(512)S(1)} %add_rsqrt_fusion), kind=kOutput, calls=%fused_computation.17 | convolution fusion | flops 3228827648 | bytes 12068864 | tf_op jit(solution)/shard_map/dot_general | solution.py:66
  250.1 3.1 %copy.242 = bf16[64,4,8,512]{3,2,0,1:T(8,128)(2,1)} copy(bf16[64,4,8,512]{3,2,1,0:T(8,128)(2,1)} %bitcast.220) | data formatting | bytes 4194304 | tf_op jit(solution)/shard_map/reshape | solution.py:76
  253.2 4.5 %all-to-all-start.1 = ((bf16[512,4,512]{2,0,1:T(8,128)(2,1)}), bf16[512,4,512]{2,0,1:T(8,128)(2,1)}, u32[]{:S(2)}, u32[]{:S(2)}) async-start(bf16[512,4,512]{2,0,1:T(8,128)(2,1)} %bitcast.215), calls=%async_computation.1 | async-start | bytes 4194304 | tf_op jit(solution)/shard_map/all_to_all | solution.py:77
  258.6 25.8 %all-to-all-done.1 = bf16[512,4,512]{2,0,1:T(8,128)(2,1)} async-done(((bf16[512,4,512]{2,0,1:T(8,128)(2,1)}), bf16[512,4,512]{2,0,1:T(8,128)(2,1)}, u32[]{:S(2)}, u32[]{:S(2)}) %all-to-all-start.1) | async-done | bytes 2097184 | tf_op jit(solution)/shard_map/all_to_all | solution.py:77
  (164 shorter events, 55.9 us)
Async XLA Ops:
  7.2 234.7 %copy-start = (bf16[768,2048]{1,0:T(8,128)(2,1)S(1)}, bf16[768,2048]{1,0:T(8,128)(2,1)}, u32[]{:S(2)}) copy-start(bf16[768,2048]{1,0:T(8,128)(2,1)} %param.27) | copy-start | bytes 9437188
  7.2 38.3 %copy-start.22 = (f32[2048]{0:T(1024)S(1)}, f32[2048]{0:T(1024)}, u32[]{:S(2)}) copy-start(f32[2048]{0:T(1024)} %param.17) | copy-start | bytes 24580
  7.2 38.3 %copy-start.23 = (f32[512]{0:T(512)S(1)}, f32[512]{0:T(512)}, u32[]{:S(2)}) copy-start(f32[512]{0:T(512)} %param.22) | copy-start | bytes 6148
  7.2 36.1 %all-gather.5.cloned.1.call-start = ((), (), s32[]{:S(2)}) async-start(), calls=%async_computation.2 | async-start | bytes 2621440 | tf_op jit(solution)/shard_map/all_gather | solution.py:70
  7.9 147.3 %all-gather.9.cloned.1.call-start = ((), (), s32[]{:S(2)}) async-start(), calls=%async_computation.4 | async-start | bytes 4595712 | tf_op jit(solution)/shard_map/all_gather | solution.py:25
  62.7 6.2 %copy-start.21 = (bf16[2048,512]{1,0:T(8,128)(2,1)S(1)}, bf16[2048,512]{1,0:T(8,128)(2,1)}, u32[]{:S(2)}) copy-start(bf16[2048,512]{1,0:T(8,128)(2,1)} %param.20) | copy-start | bytes 6291460
  68.8 32.7 %copy-start.17 = (f32[8,4,128]{2,1,0:T(4,128)}, f32[8,4,128]{2,1,0:T(4,128)S(1)}, u32[]{:S(2)}) copy-start(f32[8,4,128]{2,1,0:T(4,128)S(1)} %get-tuple-element.56) | copy-start | bytes 49156
  77.5 8.9 %copy-start.20 = (s32[4,2]{0,1:T(2,128)S(1)}, s32[4,2]{0,1:T(2,128)}, u32[]{:S(2)}) copy-start(s32[4,2]{0,1:T(2,128)} %param.15) | copy-start | bytes 100
  80.3 154.3 %all-gather.7.cloned.1.call-start = ((), (), s32[]{:S(2)}) async-start(), calls=%async_computation.3 | async-start | bytes 2621440 | tf_op jit(solution)/shard_map/all_gather | solution.py:70
  85.1 12.1 %copy-start.2 = (f32[8,4,128,128]{3,2,1,0:T(8,128)S(1)}, f32[8,4,128,128]{3,2,1,0:T(8,128)}, u32[]{:S(2)}) copy-start(f32[8,4,128,128]{3,2,1,0:T(8,128)} %copy-done.1) | copy-start | bytes 6291460
  98.3 30.4 %copy-start.7 = (f32[8,4,128,128]{3,2,1,0:T(8,128)}, f32[8,4,128,128]{3,2,1,0:T(8,128)S(1)}, u32[]{:S(2)}) copy-start(f32[8,4,128,128]{3,2,1,0:T(8,128)S(1)} %add_dynamic-update-slice_fusion) | copy-start | bytes 6291460
  100.7 9.4 %collective-permute-start.2 = (bf16[2,4,130,128]{3,2,1,0:T(8,128)(2,1)S(1)}, bf16[2,4,130,128]{3,2,1,0:T(8,128)(2,1)S(1)}, u32[]{:S(2)}, u32[]{:S(2)}) collective-permute-start(bf16[2,4,130,128]{3,2,1,0:T(8,128)(2,1)S(1)} %broadcast_select_fusion), channel_id=1, source_target_pairs={{0,4},{4,8},{8,12},{12,16},{16,20},{20,24},{24,28},{28,32},{32,36}... | collective-permute-start | bytes 798728 | tf_op jit(solution)/shard_map/ppermute | solution.py:51
  110.2 17.8 %collective-permute-start.3 = (bf16[2,4,130,128]{3,2,1,0:T(8,128)(2,1)S(1)}, bf16[2,4,130,128]{3,2,1,0:T(8,128)(2,1)S(1)}, u32[]{:S(2)}, u32[]{:S(2)}) collective-permute-start(bf16[2,4,130,128]{3,2,1,0:T(8,128)(2,1)S(1)} %get-tuple-element.19), channel_id=1, source_target_pairs={{0,8},{4,12},{8,16},{12,20},{16,24},{20,28},{24,32},{28,36},{32,40... | collective-permute-start | bytes 798728 | tf_op jit(solution)/shard_map/ppermute | solution.py:51
  110.4 36.5 %copy-start.4 = (f32[8,64,4,128]{3,0,1,2:T(8,128)S(1)}, f32[8,64,4,128]{3,0,1,2:T(8,128)}, u32[]{:S(2)}) copy-start(f32[8,64,4,128]{3,0,1,2:T(8,128)} %get-tuple-element.37) | copy-start | bytes 3145732
  110.4 36.5 %copy-start.6 = (f32[8,64,4,128]{3,0,1,2:T(8,128)S(1)}, f32[8,64,4,128]{3,0,1,2:T(8,128)}, u32[]{:S(2)}) copy-start(f32[8,64,4,128]{3,0,1,2:T(8,128)} %get-tuple-element.36) | copy-start | bytes 3145732
  110.4 44.8 %collective-permute-start = (bf16[4,130,128]{2,1,0:T(8,128)(2,1)S(1)}, bf16[4,130,128]{2,1,0:T(8,128)(2,1)S(1)}, u32[]{:S(2)}, u32[]{:S(2)}) collective-permute-start(bf16[4,130,128]{2,1,0:T(8,128)(2,1)S(1)} %maximum_select_fusion), channel_id=1, source_target_pairs={{0,124},{4,0},{8,4},{12,8},{16,12},{20,16},{24,20},{28,24},{32,28}... | collective-permute-start | bytes 399368 | tf_op jit(solution)/shard_map/ppermute | solution.py:41
  128.1 10.4 %collective-permute-start.4 = (bf16[2,4,130,128]{3,2,1,0:T(8,128)(2,1)S(1)}, bf16[2,4,130,128]{3,2,1,0:T(8,128)(2,1)S(1)}, u32[]{:S(2)}, u32[]{:S(2)}) collective-permute-start(bf16[2,4,130,128]{3,2,1,0:T(8,128)(2,1)S(1)} %broadcast_select_fusion.2), channel_id=1, source_target_pairs={{0,16},{4,20},{8,24},{12,28},{16,32},{20,36},{24,40},{28,44},{32,4... | collective-permute-start | bytes 798728 | tf_op jit(solution)/shard_map/ppermute | solution.py:51
  138.6 7.8 %collective-permute-start.5 = (bf16[2,4,130,128]{3,2,1,0:T(8,128)(2,1)S(1)}, bf16[2,4,130,128]{3,2,1,0:T(8,128)(2,1)S(1)}, u32[]{:S(2)}, u32[]{:S(2)}) collective-permute-start(bf16[2,4,130,128]{3,2,1,0:T(8,128)(2,1)S(1)} %get-tuple-element.12), channel_id=1, source_target_pairs={{0,32},{4,36},{8,40},{12,44},{16,48},{20,52},{24,56},{28,60},{32,6... | collective-permute-start | bytes 798728 | tf_op jit(solution)/shard_map/ppermute | solution.py:51
  138.8 16.4 %collective-permute-start.1 = (bf16[4,130,128]{2,1,0:T(8,128)(2,1)S(1)}, bf16[4,130,128]{2,1,0:T(8,128)(2,1)S(1)}, u32[]{:S(2)}, u32[]{:S(2)}) collective-permute-start(bf16[4,130,128]{2,1,0:T(8,128)(2,1)S(1)} %maximum_select_fusion.1), channel_id=1, source_target_pairs={{124,60},{125,61},{126,62},{127,63}} | collective-permute-start | bytes 399368 | tf_op jit(solution)/shard_map/ppermute | solution.py:42
  146.6 8.4 %collective-permute-start.6 = (bf16[2,4,130,128]{3,2,1,0:T(8,128)(2,1)S(1)}, bf16[2,4,130,128]{3,2,1,0:T(8,128)(2,1)S(1)}, u32[]{:S(2)}, u32[]{:S(2)}) collective-permute-start(bf16[2,4,130,128]{3,2,1,0:T(8,128)(2,1)S(1)} %broadcast_select_fusion.4), channel_id=1, source_target_pairs={{0,64},{4,68},{8,72},{12,76},{16,80},{20,84},{24,88},{28,92},{32,9... | collective-permute-start | bytes 798728 | tf_op jit(solution)/shard_map/ppermute | solution.py:51
  157.6 7.7 %copy-start.5 = (f32[8,64,4,128]{3,0,1,2:T(8,128)S(1)}, f32[8,64,4,128]{3,0,1,2:T(8,128)}, u32[]{:S(2)}) copy-start(f32[8,64,4,128]{3,0,1,2:T(8,128)} %get-tuple-element.37) | copy-start | bytes 3145732
  157.6 7.7 %copy-start.8 = (f32[8,4,128,128]{3,2,1,0:T(8,128)S(1)}, f32[8,4,128,128]{3,2,1,0:T(8,128)}, u32[]{:S(2)}) copy-start(f32[8,4,128,128]{3,2,1,0:T(8,128)} %copy-done.7) | copy-start | bytes 6291460
  157.7 7.7 %copy-start.18 = (f32[8,4,128]{2,1,0:T(4,128)S(1)}, f32[8,4,128]{2,1,0:T(4,128)}, u32[]{:S(2)}) copy-start(f32[8,4,128]{2,1,0:T(4,128)} %copy-done.17) | copy-start | bytes 49156
  253.2 31.1 %all-to-all-start.1 = ((bf16[512,4,512]{2,0,1:T(8,128)(2,1)}), bf16[512,4,512]{2,0,1:T(8,128)(2,1)}, u32[]{:S(2)}, u32[]{:S(2)}) async-start(bf16[512,4,512]{2,0,1:T(8,128)(2,1)} %bitcast.215), calls=%async_computation.1 | async-start | bytes 4194304 | tf_op jit(solution)/shard_map/all_to_all | solution.py:77
  (11 other events, 25.1 us)
Sparse Core Ops, SparseCore 0:
  9.7 33.5 all-gather.4
  80.4 51.8 all-gather.8
  207.1 27.4 all-gather.6
